TPU v7x, 32 devices: a whole 2x2x4 slice. The times are simulated.
32 devices in a mesh: grp: 2 (over y), blk: 8 (over z, x), tch: 2 (over core).
Axes of the slice: x: 2, y: 2, z: 4, core: 2. Of those that a mesh axis runs over, the one named last changes fastest.
Arguments:
- samples: bfloat16 [4, 32, 65536], P('grp', 'blk', 'tch'), parts along dimension 0, may hold values from -6 to 6
- history: bfloat16 [4, 32, 15360], P('grp', 'blk'), parts along dimension 0, may hold values from -6 to 6
- coefficients: float32 [16, 1024], replicated, may hold values from -1.5 to 1.5
- station_of_slot: int32 [32], P('grp'), parts along dimension 0, may hold values from 0 to 15, each once
- station_ok: int32 [32], P('grp'), parts along dimension 0, may hold values from 0 to 1, as said below
Outputs:
- visibilities: bfloat16 [4, 1024, 32, 32], P('grp', ('blk', 'tch')), parts along dimension 0
There are 2 independent parts, one for each index of `grp`. A program takes and returns all parts, laid end to end along the dimension named above; an argument that names none is the same for every part. Nothing has to cross between parts.
Inputs may be any that keep to these rules, and one draw needn't show every extreme that they name: `station_of_slot`: each station stands in exactly one slot. `station_ok`: 2 or 3 stations are flagged.
All inputs are finite; a program needn't handle non-finite values.
Results may differ from a plain program's by a relative error of at most 0.0074.
Values may be sent and summed in bfloat16 or wider, within the bound.
No kernel may reach another device: no remote copies, remote signals or barrier semaphores. Data moves between devices by JAX's collectives and lax.ppermute only.
A program may use at most 64 MiB of HBM per device.

v0:
```python
import math
import jax
import jax.numpy as jnp
from jax import lax
from jax.sharding import PartitionSpec as P

POLS = 2


def shifted(block, axis, distance):
    devices = range(lax.axis_size(axis))
    route = [(i - distance, i) for i in devices if i - distance in devices]
    return lax.ppermute(block, axis, route)


def dft_table(fft_len):
    row_index = lax.broadcasted_iota(jnp.int32, (fft_len, fft_len), 0)
    col_index = lax.broadcasted_iota(jnp.int32, (fft_len, fft_len), 1)
    phase_step = row_index * col_index % fft_len
    angles = phase_step.astype(jnp.float32) * (2.0 * math.pi / fft_len)
    norm_scale = 1.0 / math.sqrt(fft_len)
    cosine = jnp.cos(angles) * norm_scale
    sine_part = jnp.sin(angles) * norm_scale
    upper_half = jnp.concatenate([cosine, -sine_part], axis=1)
    lower_half = jnp.concatenate([sine_part, cosine], axis=1)
    return jnp.concatenate([upper_half, lower_half], axis=0).astype(jnp.bfloat16)


def filter_bank(extended, coefficients, spec_count):
    tap_count, fft_len = coefficients.shape
    blocks = extended.reshape(extended.shape[0], extended.shape[1], -1, fft_len)
    running = jnp.zeros((extended.shape[0], extended.shape[1], spec_count, fft_len), jnp.float32)
    for tap_index in range(tap_count):
        running = running + coefficients[tap_index] * blocks[
            :, :, tap_index : tap_index + spec_count, :
        ].astype(jnp.float32)
    return running.astype(jnp.bfloat16)


def channel_major(filtered, dft_matrix):
    row_count, spec_count, fft_len = (filtered.shape[1], filtered.shape[2], filtered.shape[3])
    flat_rows = jnp.transpose(filtered, (1, 2, 0, 3)).reshape(row_count * spec_count, 2 * fft_len)
    product = jnp.dot(flat_rows, dft_matrix, preferred_element_type=jnp.float32).astype(
        jnp.bfloat16
    )
    product = product.reshape(row_count, spec_count, 2, fft_len)
    return jnp.transpose(product, (3, 0, 2, 1)).reshape(fft_len, row_count * 2 * spec_count)


def reorder_inputs(values, station_of_slot, station_ok):
    station_count = station_of_slot.shape[0]
    input_count = values.shape[1]
    slot_index = (
        jnp.zeros((station_count,), jnp.int32)
        .at[station_of_slot]
        .set(jnp.arange(station_count, dtype=jnp.int32))
    )
    position = jnp.arange(input_count, dtype=jnp.int32)
    source_rows = slot_index[position // POLS] * POLS + position % POLS
    keep_mask = station_ok[position // POLS].astype(values.dtype)
    return jnp.take(values, source_rows, axis=1) * keep_mask[None, :, None]


def rotate_parts(ordered):
    half_cols = ordered.shape[2] // 2
    return jnp.concatenate([-ordered[:, :, half_cols:], ordered[:, :, :half_cols]], axis=2)


def correlate_full(ordered, inverse_count):
    rotated = rotate_parts(ordered)
    real_vis = jnp.einsum("cak,cbk->cab", ordered, ordered, preferred_element_type=jnp.float32)
    imag_vis = jnp.einsum("cak,cbk->cab", ordered, rotated, preferred_element_type=jnp.float32)
    return (jnp.stack([real_vis, imag_vis], axis=0) * inverse_count).astype(jnp.bfloat16)


def local(samples, history, coefficients, station_of_slot, station_ok):
    tap_count, fft_len = coefficients.shape
    row_count = samples.shape[1]
    spec_local = samples.shape[2] // fft_len
    half_count = lax.axis_size("tch")
    block_count = lax.axis_size("blk")
    spec_total = spec_local * half_count
    dft_matrix = dft_table(fft_len)
    tail_block = jnp.concatenate([history, samples], axis=2)[:, :, -(tap_count - 1) * fft_len :]
    earlier = shifted(tail_block, "tch", 1)
    is_first = lax.axis_index("tch") == 0
    earlier = jnp.where(is_first, history, earlier)
    extended = jnp.concatenate([earlier, samples], axis=2)
    by_channel = channel_major(filter_bank(extended, coefficients, spec_local), dft_matrix)
    by_block = lax.all_to_all(by_channel, "blk", split_axis=0, concat_axis=1, tiled=True)
    turned = lax.all_to_all(by_block, "tch", split_axis=0, concat_axis=1, tiled=True)
    chan_local = turned.shape[0]
    layout = turned.reshape(chan_local, half_count, block_count, row_count, 2, spec_local)
    layout = jnp.transpose(layout, (0, 2, 3, 4, 1, 5))
    stacked = layout.reshape(chan_local, block_count * row_count, 2 * spec_total)
    ordered = reorder_inputs(stacked, station_of_slot, station_ok)
    inverse_count = 1.0 / spec_total
    return correlate_full(ordered, inverse_count)


def solution(mesh):
    return jax.shard_map(
        local,
        mesh=mesh,
        in_specs=(P("grp", "blk", "tch"), P("grp", "blk", None), P(), P("grp"), P("grp")),
        out_specs=P("grp", ("blk", "tch"), None, None),
        check_vma=False,
    )
```

profile of v0, /device:TPU:0, one launch (start us, length us, event | category | flops | bytes accessed | tf_op | source)
XLA Modules:
  0.0 76.3 jit_solution(1272274682949165277)
XLA Ops:
  0.0 1.0 %slice.106 = bf16[2,4,15360]{2,1,0:T(4,128)(2,1)S(1)} slice(bf16[2,4,32768]{2,1,0:T(4,128)(2,1)} %param.5), slice={[0:2], [0:4], [17408:32768]} | slice | bytes 491520 | tf_op jit(solution)/shard_map/slice | solution.py:84
  1.0 2.4 %collective-permute-start = (bf16[2,4,15360]{2,1,0:T(4,128)(2,1)S(1)}, bf16[2,4,15360]{2,1,0:T(4,128)(2,1)S(1)}, u32[]{:S(2)}, u32[]{:S(2)}) collective-permute-start(bf16[2,4,15360]{2,1,0:T(4,128)(2,1)S(1)} %slice.106), channel_id=1, source_target_pairs={{0,1},{2,3},{4,5},{6,7},{8,9},{10,11},{12,13},{14,15},{16,17},{18,... | collective-permute-start | bytes 737288 | tf_op jit(solution)/shard_map/ppermute | solution.py:13
  3.4 17.9 %negate_convert_fusion = (bf16[1024,1024]{1,0:T(8,128)(2,1)}, bf16[1024,1024]{1,0:T(8,128)(2,1)}) fusion(), kind=kLoop, calls=%fused_computation.18 | loop fusion | flops 19922944 | bytes 4194304 | tf_op jit(solution)/shard_map/convert.5
  21.4 16.6 %fusion.14 = bf16[1024,1024]{1,0:T(8,128)(2,1)} fusion(), kind=kLoop, calls=%fused_computation.24 | loop fusion | flops 16777216 | bytes 2097152 | tf_op jit(solution)/shard_map/convert.2
  38.1 0.3 pad_maximum_fusion
  38.4 0.5 reshape.130
  38.9 2.2 %fusion.25 = bf16[4,32,2,1024]{3,1,0,2:T(8,128)(2,1)S(1)} fusion(bf16[2,4,47,1024]{3,2,1,0:T(8,128)(2,1)S(1)} %reshape.130, f32[1024]{0:T(1024)S(1)} %bitcast.78, f32[1024]{0:T(1024)S(1)} %bitcast.79, f32[1024]{0:T(1024)S(1)} %bitcast.65, f32[1024]{0:T(1024)S(1)} %bitcast.66, f32[1024]{0:T(1024)S(1)} %bitcast.67, f32[1024]{0:T(1024)S(1)} %bitcast.68, ...), kind=kLoop, calls=%fused_computation.38 | loop fusion | flops 12582912 | bytes 8978432 | tf_op jit(solution)/shard_map/transpose | solution.py:42
  41.2 0.5 copy.24
  41.7 0.1 copy.34
  41.9 0.9 %copy-done.1 = bf16[1024,1024]{1,0:T(8,128)(2,1)S(1)} copy-done((bf16[1024,1024]{1,0:T(8,128)(2,1)S(1)}, bf16[1024,1024]{1,0:T(8,128)(2,1)}, u32[]{:S(2)}) %copy-start.1) | copy-done | bytes 2097176
  42.7 1.3 %fusion.15 = bf16[128,2048]{1,0:T(8,128)(2,1)S(1)} fusion(bf16[128,2048]{1,0:T(8,128)(2,1)S(1)} %bitcast.61, bf16[1024,1024]{1,0:T(8,128)(2,1)S(1)} %copy-done.2, bf16[1024,1024]{1,0:T(8,128)(2,1)S(1)} %copy-done.3, bf16[1024,1024]{1,0:T(8,128)(2,1)S(1)} %copy-done.1), kind=kOutput, calls=%fused_computation.25 | convolution fusion | flops 1107558400 | bytes 7340032 | tf_op jit(solution)/shard_map/dot_general | solution.py:43
  44.0 0.4 reshape.132
  44.6 0.9 %copy.26 = bf16[8,128,256]{1,2,0:T(8,128)(2,1)} copy(bf16[8,128,256]{1,0,2:T(8,128)(2,1)S(1)} %bitcast.59) | data formatting | bytes 1048576 | tf_op jit(solution)/shard_map/all_to_all | solution.py:90
  45.5 6.6 %all-to-all-start = ((bf16[8,128,256]{1,2,0:T(8,128)(2,1)}), bf16[8,128,256]{1,2,0:T(8,128)(2,1)S(1)}, u32[]{:S(2)}, u32[]{:S(2)}) async-start(bf16[8,128,256]{1,2,0:T(8,128)(2,1)} %copy.26), calls=%async_computation | async-start | bytes 1048576 | tf_op jit(solution)/shard_map/all_to_all | solution.py:90
  52.2 0.6 scatter_custom_fusion
  52.8 0.7 gather_fusion
  53.5 0.7 gather_fusion.2
  54.3 11.9 %all-to-all-done = bf16[8,128,256]{1,2,0:T(8,128)(2,1)S(1)} async-done(((bf16[8,128,256]{1,2,0:T(8,128)(2,1)}), bf16[8,128,256]{1,2,0:T(8,128)(2,1)S(1)}, u32[]{:S(2)}, u32[]{:S(2)}) %all-to-all-start) | async-done | bytes 524320 | tf_op jit(solution)/shard_map/all_to_all | solution.py:90
  66.2 0.4 copy.27
  66.6 0.2 all_to_all.27
  66.9 4.2 %all_to_all.32 = bf16[2,64,2048]{2,1,0:T(8,128)(2,1)S(1)} all-to-all(bf16[2,64,2048]{2,1,0:T(8,128)(2,1)S(1)} %all_to_all.27), channel_id=1, replica_groups=mesh['grp'=2,'blk'=8,'tch'=2] {'tch'}, dimensions={0} | all-to-all | bytes 1048576 | tf_op jit(solution)/shard_map/all_to_all | solution.py:91
  71.0 0.5 copy.28
  71.5 0.1 copy.29
  71.7 0.4 copy.30
  72.1 0.7 gather_fusion.1
  72.8 0.3 fusion.24
  73.1 0.2 slice_negate_fusion
  73.4 0.4 fusion.35
  73.7 0.5 fusion.19
  74.2 0.6 copy.33
  74.8 0.6 copy.32
  75.4 0.9 %fusion.18 = bf16[2,64,32,32]{1,3,2,0:T(8,128)(2,1)} fusion(f32[1,64,32,32]{1,3,2,0:T(8,128)S(1)} %bitcast.53, f32[1,64,32,32]{1,3,2,0:T(8,128)S(1)} %bitcast.54), kind=kLoop, calls=%fused_computation.27 | loop fusion | flops 393216 | bytes 786432 | tf_op jit(solution)/shard_map/convert_element_type | solution.py:73
  (28 shorter events, 0.4 us)
Async XLA Ops:
  0.0 53.5 %copy-start = (s32[16]{0:T(128)S(1)}, s32[16]{0:T(128)}, u32[]{:S(2)}) copy-start(s32[16]{0:T(128)} %param.9) | copy-start | bytes 196
  1.0 36.9 %collective-permute-start = (bf16[2,4,15360]{2,1,0:T(4,128)(2,1)S(1)}, bf16[2,4,15360]{2,1,0:T(4,128)(2,1)S(1)}, u32[]{:S(2)}, u32[]{:S(2)}) collective-permute-start(bf16[2,4,15360]{2,1,0:T(4,128)(2,1)S(1)} %slice.106), channel_id=1, source_target_pairs={{0,1},{2,3},{4,5},{6,7},{8,9},{10,11},{12,13},{14,15},{16,17},{18,... | collective-permute-start | bytes 737288 | tf_op jit(solution)/shard_map/ppermute | solution.py:13
  21.4 16.6 %copy-start.6 = (f32[16,1024]{1,0:T(8,128)S(1)}, f32[16,1024]{1,0:T(8,128)}, u32[]{:S(2)}) copy-start(f32[16,1024]{1,0:T(8,128)} %param.7) | copy-start | bytes 196612
  21.4 16.6 %copy-start.5 = (bf16[2,4,15360]{2,1,0:T(4,128)(2,1)S(1)}, bf16[2,4,15360]{2,1,0:T(4,128)(2,1)}, u32[]{:S(2)}) copy-start(bf16[2,4,15360]{2,1,0:T(4,128)(2,1)} %param.6) | copy-start | bytes 737284
  21.4 16.7 %copy-start.4 = (bf16[2,4,32768]{2,1,0:T(4,128)(2,1)S(1)}, bf16[2,4,32768]{2,1,0:T(4,128)(2,1)}, u32[]{:S(2)}) copy-start(bf16[2,4,32768]{2,1,0:T(4,128)(2,1)} %param.5) | copy-start | bytes 1572868
  38.9 2.9 %copy-start.2 = (bf16[1024,1024]{1,0:T(8,128)(2,1)S(1)}, bf16[1024,1024]{1,0:T(8,128)(2,1)}, u32[]{:S(2)}) copy-start(bf16[1024,1024]{1,0:T(8,128)(2,1)} %get-tuple-element.24) | copy-start | bytes 6291460
  38.9 2.9 %copy-start.3 = (bf16[1024,1024]{1,0:T(8,128)(2,1)S(1)}, bf16[1024,1024]{1,0:T(8,128)(2,1)}, u32[]{:S(2)}) copy-start(bf16[1024,1024]{1,0:T(8,128)(2,1)} %fusion.14) | copy-start | bytes 6291460
  41.2 1.6 %copy-start.1 = (bf16[1024,1024]{1,0:T(8,128)(2,1)S(1)}, bf16[1024,1024]{1,0:T(8,128)(2,1)}, u32[]{:S(2)}) copy-start(bf16[1024,1024]{1,0:T(8,128)(2,1)} %get-tuple-element.23) | copy-start | bytes 6291460
  44.4 7.8 %copy-start.7 = (s32[16]{0:T(128)S(1)}, s32[16]{0:T(128)}, u32[]{:S(2)}) copy-start(s32[16]{0:T(128)} %param.8) | copy-start | bytes 196
  45.5 20.7 %all-to-all-start = ((bf16[8,128,256]{1,2,0:T(8,128)(2,1)}), bf16[8,128,256]{1,2,0:T(8,128)(2,1)S(1)}, u32[]{:S(2)}, u32[]{:S(2)}) async-start(bf16[8,128,256]{1,2,0:T(8,128)(2,1)} %copy.26), calls=%async_computation | async-start | bytes 1048576 | tf_op jit(solution)/shard_map/all_to_all | solution.py:90
where the time goes:
time: 76.6 us; the launch traced here: 76.3 us
  other arithmetic  38.6 us (50%)
  waiting for transfers between devices  11.9 us (16%)
  local copies, waits for them, and re-layouts  10.2 us (13%)
  starting transfers between devices  9 us (12%)
  blocking collectives  4.15 us (5%)
  matrix products  2.12 us (3%)
    another operation x2, other arithmetic  34.5 us
    all_to_all x1, waiting for transfers between devices, local(): lax.all_to_all(by_channel, 'blk', split_axis=0, concat_axis=1, tiled=True)  11.9 us
    all_to_all x1, starting transfers between devices, local(): lax.all_to_all(by_channel, 'blk', split_axis=0, concat_axis=1, tiled=True)  6.63 us
    all_to_all x1, blocking collectives, local(): lax.all_to_all(by_block, 'tch', split_axis=0, concat_axis=1, tiled=True)  4.15 us
    ppermute x1, starting transfers between devices, shifted(): return lax.ppermute(block, axis, route)  2.37 us
    transpose x1, other arithmetic, channel_major(): jnp.transpose(filtered, (1, 2, 0, 3))  2.23 us
  transfers between devices with their start and end apart: 2, of which 1 were waited for; matrix products, arithmetic and copies ran while one was open for 48% of the time, Pallas kernels for 0%

commit v1 on v0

--- a/solution.py
+++ b/solution.py
@@ -5,6 +5,17 @@
 from jax.sharding import PartitionSpec as P
 
 POLS = 2
+
+
+def split_up(x, dim, size):
+    before, after = (x.shape[:dim], x.shape[dim + 1 :])
+    return jnp.moveaxis(x.reshape(*before, size, -1, *after), dim, 0)
+
+
+def joined_along(tiles, dim):
+    tiles = jnp.moveaxis(tiles, 0, dim)
+    lengths = tiles.shape
+    return tiles.reshape(*lengths[:dim], lengths[dim] * lengths[dim + 1], *lengths[dim + 2 :])
 
 
 def shifted(block, axis, distance):
@@ -87,7 +98,17 @@
     earlier = jnp.where(is_first, history, earlier)
     extended = jnp.concatenate([earlier, samples], axis=2)
     by_channel = channel_major(filter_bank(extended, coefficients, spec_local), dft_matrix)
-    by_block = lax.all_to_all(by_channel, "blk", split_axis=0, concat_axis=1, tiled=True)
+    size, index = (lax.axis_size("blk"), lax.axis_index("blk"))
+    pieces = split_up(by_channel, 0, size)
+    result = pieces
+    for step in range(1, size):
+        target, source = ((index + step) % size, (index - step) % size)
+        sent = lax.dynamic_index_in_dim(pieces, target, 0)
+        partner_block = lax.ppermute(
+            sent, "blk", [(i_2, (i_2 + step) % size) for i_2 in range(size)]
+        )
+        result = lax.dynamic_update_slice_in_dim(result, partner_block, source, axis=0)
+    by_block = joined_along(result, 1)
     turned = lax.all_to_all(by_block, "tch", split_axis=0, concat_axis=1, tiled=True)
     chan_local = turned.shape[0]
     layout = turned.reshape(chan_local, half_count, block_count, row_count, 2, spec_local)

time: 76.6 us -> 99 us (1.29)
  the two profiles are of different devices: /device:TPU:0 before, /device:TPU:25 now
where the time goes in v1:
time: 99 us; the launch traced here: 98.8 us
  other arithmetic  38.6 us (39%)
  local copies, waits for them, and re-layouts  30.2 us (31%)
  blocking collectives  11.2 us (11%)
  starting transfers between devices  8.48 us (9%)
  waiting for transfers between devices  7.53 us (8%)
  matrix products  2.12 us (2%)
    another operation x2, other arithmetic  34.5 us
    dynamic_update_slice x7, local copies, waits for them, and re-layouts, local(): lax.dynamic_update_slice_in_dim(result, partner_block, source, axis=0)  19.7 us
    all_to_all x1, blocking collectives, local(): lax.all_to_all(by_block, 'tch', split_axis=0, concat_axis=1, tiled=True)  11.2 us
    ppermute x7, waiting for transfers between devices, local(): lax.ppermute(sent, 'blk', [(i_2, (i_2 + step) % size) for i_2 in range(si...  7.53 us
    ppermute x7, starting transfers between devices, local(): lax.ppermute(sent, 'blk', [(i_2, (i_2 + step) % size) for i_2 in range(si...  7.18 us
    transpose x1, other arithmetic, channel_major(): jnp.transpose(filtered, (1, 2, 0, 3))  2.23 us
  transfers between devices with their start and end apart: 8, of which 1 were waited for; matrix products, arithmetic and copies ran while one was open for 54% of the time, Pallas kernels for 0%

profile of v1, /device:TPU:25, one launch (start us, length us, event | category | flops | bytes accessed | tf_op | source)
XLA Modules:
  0.0 98.8 jit_solution(910680242159001023)
XLA Ops:
  0.0 1.0 %slice.106 = bf16[2,4,15360]{2,1,0:T(4,128)(2,1)S(1)} slice(bf16[2,4,32768]{2,1,0:T(4,128)(2,1)} %param.5), slice={[0:2], [0:4], [17408:32768]} | slice | bytes 491520 | tf_op jit(solution)/shard_map/slice | solution.py:95
  1.0 1.3 %collective-permute-start = (bf16[2,4,15360]{2,1,0:T(4,128)(2,1)S(1)}, bf16[2,4,15360]{2,1,0:T(4,128)(2,1)S(1)}, u32[]{:S(2)}, u32[]{:S(2)}) collective-permute-start(bf16[2,4,15360]{2,1,0:T(4,128)(2,1)S(1)} %slice.106), channel_id=1, source_target_pairs={{0,1},{2,3},{4,5},{6,7},{8,9},{10,11},{12,13},{14,15},{16,17},{18,... | collective-permute-start | bytes 737288 | tf_op jit(solution)/shard_map/ppermute | solution.py:24
  2.3 17.9 %negate_convert_fusion = (bf16[1024,1024]{1,0:T(8,128)(2,1)}, bf16[1024,1024]{1,0:T(8,128)(2,1)}) fusion(), kind=kLoop, calls=%fused_computation.18 | loop fusion | flops 19922944 | bytes 4194304 | tf_op jit(solution)/shard_map/convert.5
  20.3 16.6 %fusion.14 = bf16[1024,1024]{1,0:T(8,128)(2,1)} fusion(), kind=kLoop, calls=%fused_computation.24 | loop fusion | flops 16777216 | bytes 2097152 | tf_op jit(solution)/shard_map/convert.2
  36.9 0.6 scatter_custom_fusion
  37.6 0.7 gather_fusion
  38.8 0.5 reshape.126
  39.4 2.2 %fusion.25 = bf16[4,32,2,1024]{3,1,0,2:T(8,128)(2,1)S(1)} fusion(bf16[2,4,47,1024]{3,2,1,0:T(8,128)(2,1)S(1)} %reshape.126, f32[1024]{0:T(1024)S(1)} %bitcast.79, f32[1024]{0:T(1024)S(1)} %bitcast.80, f32[1024]{0:T(1024)S(1)} %bitcast.66, f32[1024]{0:T(1024)S(1)} %bitcast.67, f32[1024]{0:T(1024)S(1)} %bitcast.68, f32[1024]{0:T(1024)S(1)} %bitcast.69, ...), kind=kLoop, calls=%fused_computation.38 | loop fusion | flops 12582912 | bytes 8978432 | tf_op jit(solution)/shard_map/transpose | solution.py:53
  41.6 0.5 copy.15
  42.3 0.9 copy-done.1
  43.2 1.3 %fusion.15 = bf16[128,2048]{1,0:T(8,128)(2,1)S(1)} fusion(bf16[128,2048]{1,0:T(8,128)(2,1)S(1)} %bitcast.62, bf16[1024,1024]{1,0:T(8,128)(2,1)S(1)} %copy-done.2, bf16[1024,1024]{1,0:T(8,128)(2,1)S(1)} %copy-done.3, bf16[1024,1024]{1,0:T(8,128)(2,1)S(1)} %copy-done.1), kind=kOutput, calls=%fused_computation.25 | convolution fusion | flops 1107558400 | bytes 7340032 | tf_op jit(solution)/shard_map/dot_general | solution.py:54
  45.1 1.0 constant_dynamic-slice_fusion
  46.0 1.3 %collective-permute-start.1 = (bf16[1,128,256]{1,0,2:T(2,128)(2,1)S(1)}, bf16[1,128,256]{1,0,2:T(2,128)(2,1)S(1)}, u32[]{:S(2)}, u32[]{:S(2)}) collective-permute-start(bf16[1,128,256]{1,0,2:T(2,128)(2,1)S(1)} %get-tuple-element.13), channel_id=1, source_target_pairs={{0,2},{2,4},{4,6},{6,8},{8,10},{10,12},{12,14},{14,0},{1,3},{3,5},... | collective-permute-start | bytes 196616 | tf_op jit(solution)/shard_map/ppermute | solution.py:107
  47.4 0.7 gather_fusion.2
  48.2 2.1 %collective-permute-start.3 = (bf16[1,128,256]{1,0,2:T(2,128)(2,1)S(1)}, bf16[1,128,256]{1,0,2:T(2,128)(2,1)S(1)}, u32[]{:S(2)}, u32[]{:S(2)}) collective-permute-start(bf16[1,128,256]{1,0,2:T(2,128)(2,1)S(1)} %get-tuple-element.11), channel_id=1, source_target_pairs={{0,6},{2,8},{4,10},{6,12},{8,14},{10,0},{12,2},{14,4},{1,7},{3,9},... | collective-permute-start | bytes 196616 | tf_op jit(solution)/shard_map/ppermute | solution.py:107
  50.6 2.1 %collective-permute-start.5 = (bf16[1,128,256]{1,0,2:T(2,128)(2,1)S(1)}, bf16[1,128,256]{1,0,2:T(2,128)(2,1)S(1)}, u32[]{:S(2)}, u32[]{:S(2)}) collective-permute-start(bf16[1,128,256]{1,0,2:T(2,128)(2,1)S(1)} %get-tuple-element.9), channel_id=1, source_target_pairs={{0,10},{2,12},{4,14},{6,0},{8,2},{10,4},{12,6},{14,8},{1,11},{3,13... | collective-permute-start | bytes 196616 | tf_op jit(solution)/shard_map/ppermute | solution.py:107
  52.9 1.2 %collective-permute-start.7 = (bf16[1,128,256]{1,0,2:T(2,128)(2,1)S(1)}, bf16[1,128,256]{1,0,2:T(2,128)(2,1)S(1)}, u32[]{:S(2)}, u32[]{:S(2)}) collective-permute-start(bf16[1,128,256]{1,0,2:T(2,128)(2,1)S(1)} %get-tuple-element.7), channel_id=1, source_target_pairs={{0,14},{2,0},{4,2},{6,4},{8,6},{10,8},{12,10},{14,12},{1,15},{3,1}... | collective-permute-start | bytes 196616 | tf_op jit(solution)/shard_map/ppermute | solution.py:107
  54.1 2.8 %dynamic_update_slice.21 = bf16[8,128,256]{1,0,2:T(8,128)(2,1)S(1)} dynamic-update-slice(bf16[8,128,256]{1,0,2:T(8,128)(2,1)S(1)} %bitcast.52, bf16[1,128,256]{1,0,2:T(2,128)(2,1)S(1)} %collective-permute-done.1, s32[]{:T(128)S(6)} %select_n.200, s32[]{:T(128)} %constant.160.clone.1, s32[]{:T(128)} %constant.160.clone.1) | dynamic-update-slice | bytes 131076 | tf_op jit(solution)/shard_map/dynamic_update_slice | solution.py:110
  56.9 2.8 %dynamic_update_slice.22 = bf16[8,128,256]{1,0,2:T(8,128)(2,1)S(1)} dynamic-update-slice(bf16[8,128,256]{1,0,2:T(8,128)(2,1)S(1)} %dynamic_update_slice.21, bf16[1,128,256]{1,0,2:T(2,128)(2,1)S(1)} %collective-permute-done.2, s32[]{:T(128)S(6)} %select_n.204, s32[]{:T(128)} %constant.160.clone.1, s32[]{:T(128)} %constant.160.clone.1) | dynamic-update-slice | bytes 131076 | tf_op jit(solution)/shard_map/dynamic_update_slice | solution.py:110
  59.8 7.5 %collective-permute-done.3 = bf16[1,128,256]{1,0,2:T(2,128)(2,1)S(1)} collective-permute-done((bf16[1,128,256]{1,0,2:T(2,128)(2,1)S(1)}, bf16[1,128,256]{1,0,2:T(2,128)(2,1)S(1)}, u32[]{:S(2)}, u32[]{:S(2)}) %collective-permute-start.3) | collective-permute-done | bytes 65568 | tf_op jit(solution)/shard_map/ppermute | solution.py:107
  67.3 2.8 %dynamic_update_slice.23 = bf16[8,128,256]{1,0,2:T(8,128)(2,1)S(1)} dynamic-update-slice(bf16[8,128,256]{1,0,2:T(8,128)(2,1)S(1)} %dynamic_update_slice.22, bf16[1,128,256]{1,0,2:T(2,128)(2,1)S(1)} %collective-permute-done.3, s32[]{:T(128)S(6)} %select_n.208, s32[]{:T(128)} %constant.160.clone.1, s32[]{:T(128)} %constant.160.clone.1) | dynamic-update-slice | bytes 131076 | tf_op jit(solution)/shard_map/dynamic_update_slice | solution.py:110
  70.1 2.8 %dynamic_update_slice.24 = bf16[8,128,256]{1,0,2:T(8,128)(2,1)S(1)} dynamic-update-slice(bf16[8,128,256]{1,0,2:T(8,128)(2,1)S(1)} %dynamic_update_slice.23, bf16[1,128,256]{1,0,2:T(2,128)(2,1)S(1)} %collective-permute-done.4, s32[]{:T(128)S(6)} %select_n.212, s32[]{:T(128)} %constant.160.clone.1, s32[]{:T(128)} %constant.160.clone.1) | dynamic-update-slice | bytes 131076 | tf_op jit(solution)/shard_map/dynamic_update_slice | solution.py:110
  72.9 2.8 %dynamic_update_slice.25 = bf16[8,128,256]{1,0,2:T(8,128)(2,1)S(1)} dynamic-update-slice(bf16[8,128,256]{1,0,2:T(8,128)(2,1)S(1)} %dynamic_update_slice.24, bf16[1,128,256]{1,0,2:T(2,128)(2,1)S(1)} %collective-permute-done.5, s32[]{:T(128)S(6)} %select_n.216, s32[]{:T(128)} %constant.160.clone.1, s32[]{:T(128)} %constant.160.clone.1) | dynamic-update-slice | bytes 131076 | tf_op jit(solution)/shard_map/dynamic_update_slice | solution.py:110
  75.8 2.8 %dynamic_update_slice.26 = bf16[8,128,256]{1,0,2:T(8,128)(2,1)S(1)} dynamic-update-slice(bf16[8,128,256]{1,0,2:T(8,128)(2,1)S(1)} %dynamic_update_slice.25, bf16[1,128,256]{1,0,2:T(2,128)(2,1)S(1)} %collective-permute-done.6, s32[]{:T(128)S(6)} %select_n.220, s32[]{:T(128)} %constant.160.clone.1, s32[]{:T(128)} %constant.160.clone.1) | dynamic-update-slice | bytes 131076 | tf_op jit(solution)/shard_map/dynamic_update_slice | solution.py:110
  78.6 2.8 %dynamic_update_slice.27 = bf16[8,128,256]{1,0,2:T(8,128)(2,1)S(1)} dynamic-update-slice(bf16[8,128,256]{1,0,2:T(8,128)(2,1)S(1)} %dynamic_update_slice.26, bf16[1,128,256]{1,0,2:T(2,128)(2,1)S(1)} %collective-permute-done.7, s32[]{:T(128)S(6)} %select_n.224, s32[]{:T(128)} %constant.160.clone.1, s32[]{:T(128)} %constant.160.clone.1) | dynamic-update-slice | bytes 131076 | tf_op jit(solution)/shard_map/dynamic_update_slice | solution.py:110
  81.4 0.6 copy.17
  82.3 11.2 %all_to_all.16 = bf16[2,64,2048]{2,1,0:T(8,128)(2,1)S(1)} all-to-all(bf16[2,64,2048]{2,1,0:T(8,128)(2,1)S(1)} %all_to_all.12), channel_id=1, replica_groups=mesh['grp'=2,'blk'=8,'tch'=2] {'tch'}, dimensions={0} | all-to-all | bytes 1048576 | tf_op jit(solution)/shard_map/all_to_all | solution.py:112
  93.5 0.5 copy.18
  94.6 0.7 gather_fusion.1
  96.7 0.6 copy.23
  97.3 0.6 copy.22
  97.9 0.9 fusion.18
  (47 shorter events, 3.9 us)
Async XLA Ops:
  0.0 47.4 %copy-start = (s32[16]{0:T(128)S(1)}, s32[16]{0:T(128)}, u32[]{:S(2)}) copy-start(s32[16]{0:T(128)} %param.9) | copy-start | bytes 196
  1.0 37.4 %collective-permute-start = (bf16[2,4,15360]{2,1,0:T(4,128)(2,1)S(1)}, bf16[2,4,15360]{2,1,0:T(4,128)(2,1)S(1)}, u32[]{:S(2)}, u32[]{:S(2)}) collective-permute-start(bf16[2,4,15360]{2,1,0:T(4,128)(2,1)S(1)} %slice.106), channel_id=1, source_target_pairs={{0,1},{2,3},{4,5},{6,7},{8,9},{10,11},{12,13},{14,15},{16,17},{18,... | collective-permute-start | bytes 737288 | tf_op jit(solution)/shard_map/ppermute | solution.py:24
  20.3 16.6 %copy-start.7 = (s32[16]{0:T(128)S(1)}, s32[16]{0:T(128)}, u32[]{:S(2)}) copy-start(s32[16]{0:T(128)} %param.8) | copy-start | bytes 196
  20.3 18.1 %copy-start.6 = (f32[16,1024]{1,0:T(8,128)S(1)}, f32[16,1024]{1,0:T(8,128)}, u32[]{:S(2)}) copy-start(f32[16,1024]{1,0:T(8,128)} %param.7) | copy-start | bytes 196612
  20.3 18.1 %copy-start.5 = (bf16[2,4,15360]{2,1,0:T(4,128)(2,1)S(1)}, bf16[2,4,15360]{2,1,0:T(4,128)(2,1)}, u32[]{:S(2)}) copy-start(bf16[2,4,15360]{2,1,0:T(4,128)(2,1)} %param.6) | copy-start | bytes 737284
  20.3 18.2 %copy-start.4 = (bf16[2,4,32768]{2,1,0:T(4,128)(2,1)S(1)}, bf16[2,4,32768]{2,1,0:T(4,128)(2,1)}, u32[]{:S(2)}) copy-start(bf16[2,4,32768]{2,1,0:T(4,128)(2,1)} %param.5) | copy-start | bytes 1572868
  39.3 2.9 %copy-start.2 = (bf16[1024,1024]{1,0:T(8,128)(2,1)S(1)}, bf16[1024,1024]{1,0:T(8,128)(2,1)}, u32[]{:S(2)}) copy-start(bf16[1024,1024]{1,0:T(8,128)(2,1)} %get-tuple-element.31) | copy-start | bytes 6291460
  39.4 2.9 %copy-start.3 = (bf16[1024,1024]{1,0:T(8,128)(2,1)S(1)}, bf16[1024,1024]{1,0:T(8,128)(2,1)}, u32[]{:S(2)}) copy-start(bf16[1024,1024]{1,0:T(8,128)(2,1)} %fusion.14) | copy-start | bytes 6291460
  41.6 1.6 %copy-start.1 = (bf16[1024,1024]{1,0:T(8,128)(2,1)S(1)}, bf16[1024,1024]{1,0:T(8,128)(2,1)}, u32[]{:S(2)}) copy-start(bf16[1024,1024]{1,0:T(8,128)(2,1)} %get-tuple-element.30) | copy-start | bytes 6291460
  46.0 6.7 %collective-permute-start.1 = (bf16[1,128,256]{1,0,2:T(2,128)(2,1)S(1)}, bf16[1,128,256]{1,0,2:T(2,128)(2,1)S(1)}, u32[]{:S(2)}, u32[]{:S(2)}) collective-permute-start(bf16[1,128,256]{1,0,2:T(2,128)(2,1)S(1)} %get-tuple-element.13), channel_id=1, source_target_pairs={{0,2},{2,4},{4,6},{6,8},{8,10},{10,12},{12,14},{14,0},{1,3},{3,5},... | collective-permute-start | bytes 196616 | tf_op jit(solution)/shard_map/ppermute | solution.py:107
  47.3 5.6 %collective-permute-start.2 = (bf16[1,128,256]{1,0,2:T(2,128)(2,1)S(1)}, bf16[1,128,256]{1,0,2:T(2,128)(2,1)S(1)}, u32[]{:S(2)}, u32[]{:S(2)}) collective-permute-start(bf16[1,128,256]{1,0,2:T(2,128)(2,1)S(1)} %get-tuple-element.12), channel_id=1, source_target_pairs={{0,4},{2,6},{4,8},{6,10},{8,12},{10,14},{12,0},{14,2},{1,5},{3,7},... | collective-permute-start | bytes 196616 | tf_op jit(solution)/shard_map/ppermute | solution.py:107
  48.2 19.1 %collective-permute-start.3 = (bf16[1,128,256]{1,0,2:T(2,128)(2,1)S(1)}, bf16[1,128,256]{1,0,2:T(2,128)(2,1)S(1)}, u32[]{:S(2)}, u32[]{:S(2)}) collective-permute-start(bf16[1,128,256]{1,0,2:T(2,128)(2,1)S(1)} %get-tuple-element.11), channel_id=1, source_target_pairs={{0,6},{2,8},{4,10},{6,12},{8,14},{10,0},{12,2},{14,4},{1,7},{3,9},... | collective-permute-start | bytes 196616 | tf_op jit(solution)/shard_map/ppermute | solution.py:107
  50.3 19.8 %collective-permute-start.4 = (bf16[1,128,256]{1,0,2:T(2,128)(2,1)S(1)}, bf16[1,128,256]{1,0,2:T(2,128)(2,1)S(1)}, u32[]{:S(2)}, u32[]{:S(2)}) collective-permute-start(bf16[1,128,256]{1,0,2:T(2,128)(2,1)S(1)} %get-tuple-element.10), channel_id=1, source_target_pairs={{0,8},{2,10},{4,12},{6,14},{8,0},{10,2},{12,4},{14,6},{1,9},{3,11}... | collective-permute-start | bytes 196616 | tf_op jit(solution)/shard_map/ppermute | solution.py:107
  50.6 22.3 %collective-permute-start.5 = (bf16[1,128,256]{1,0,2:T(2,128)(2,1)S(1)}, bf16[1,128,256]{1,0,2:T(2,128)(2,1)S(1)}, u32[]{:S(2)}, u32[]{:S(2)}) collective-permute-start(bf16[1,128,256]{1,0,2:T(2,128)(2,1)S(1)} %get-tuple-element.9), channel_id=1, source_target_pairs={{0,10},{2,12},{4,14},{6,0},{8,2},{10,4},{12,6},{14,8},{1,11},{3,13... | collective-permute-start | bytes 196616 | tf_op jit(solution)/shard_map/ppermute | solution.py:107
  52.7 23.0 %collective-permute-start.6 = (bf16[1,128,256]{1,0,2:T(2,128)(2,1)S(1)}, bf16[1,128,256]{1,0,2:T(2,128)(2,1)S(1)}, u32[]{:S(2)}, u32[]{:S(2)}) collective-permute-start(bf16[1,128,256]{1,0,2:T(2,128)(2,1)S(1)} %get-tuple-element.8), channel_id=1, source_target_pairs={{0,12},{2,14},{4,0},{6,2},{8,4},{10,6},{12,8},{14,10},{1,13},{3,15... | collective-permute-start | bytes 196616 | tf_op jit(solution)/shard_map/ppermute | solution.py:107
  52.9 25.7 %collective-permute-start.7 = (bf16[1,128,256]{1,0,2:T(2,128)(2,1)S(1)}, bf16[1,128,256]{1,0,2:T(2,128)(2,1)S(1)}, u32[]{:S(2)}, u32[]{:S(2)}) collective-permute-start(bf16[1,128,256]{1,0,2:T(2,128)(2,1)S(1)} %get-tuple-element.7), channel_id=1, source_target_pairs={{0,14},{2,0},{4,2},{6,4},{8,6},{10,8},{12,10},{14,12},{1,15},{3,1}... | collective-permute-start | bytes 196616 | tf_op jit(solution)/shard_map/ppermute | solution.py:107
